TPU v7x, 32 devices: a whole 2x2x4 slice. The times are simulated.
32 devices in a mesh: walk: 4 (over x, core), chol: 8 (over z, y).
Axes of the slice: x: 2, y: 2, z: 4, core: 2. Of those that a mesh axis runs over, the one named last changes fastest.
Arguments:
- old_walkers: bfloat16 [96, 2048, 128], P(('walk', 'chol'))
- half_chol: bfloat16 [16, 128, 2048], P('chol'), may hold values from -0.1875 to 0.1875
- parent: int32 [192], P(('walk', 'chol')), may hold values from -1 to 11, as said below
- field: float32 [192, 2048], P(('walk', 'chol')), may hold values from -0.8 to 0.8
Outputs:
- new_walkers: bfloat16 [192, 2048, 128], P(('walk', 'chol'))
- energy: float32 [192], P(('walk', 'chol'))
Inputs may be any that keep to these rules, and one draw needn't show every extreme that they name: `parent`: the 4 devices that share an index of chol form a column. On each device the live slots (value >= 0) come first among its 6 slots, the rest hold -1. Each column has exactly 12 live slots, every device of it at least one, and some device of it has all 6 slots live. A live value m names the walker that the column's walk index m // 3 holds as its local walker m % 3.
All inputs are finite; a program needn't handle non-finite values.
Results may differ from a plain program's by a relative error of at most 0.0062.
Values may be sent and summed in bfloat16 or wider, within the bound.
No kernel may reach another device: no remote copies, remote signals or barrier semaphores. Data moves between devices by JAX's collectives and lax.ppermute only.
A program may use at most 192 MiB of HBM per device.

v0:
```python
import jax
import jax.numpy as jnp
from jax import lax
from jax.sharding import PartitionSpec as P

ITERS = 3


def green_half(walkers):
    widened = walkers.astype(jnp.float32)
    electrons = walkers.shape[2]
    intersection = widened[:, :electrons, :]
    identity = jnp.eye(electrons, dtype=jnp.float32)
    diagonal = jnp.diagonal(intersection, axis1=1, axis2=2)
    inverse = identity[None, :, :] / diagonal[:, None, :]
    for sweep in range(ITERS):
        product = jnp.einsum("wij,wjk->wik", intersection, inverse, precision=lax.Precision.HIGHEST)
        inverse = jnp.einsum(
            "wij,wjk->wik",
            inverse,
            2.0 * identity[None, :, :] - product,
            precision=lax.Precision.HIGHEST,
        )
    theta = jnp.einsum("wnk,wkj->wnj", widened, inverse, precision=lax.Precision.HIGHEST)
    return theta.astype(jnp.bfloat16)


def block_energy(theta, vectors):
    blocks = jnp.einsum("gin,wnj->wgij", vectors, theta, preferred_element_type=jnp.float32)
    traces = jnp.einsum("wgii->wg", blocks)
    crossed = jnp.sum(blocks * jnp.swapaxes(blocks, 2, 3), axis=(2, 3))
    return 0.5 * jnp.sum(traces * traces - crossed, axis=1)


def body(old_walkers, half_chol, parent, field):
    slot_dev = parent.shape[0]
    column = lax.all_gather(old_walkers, "walk", axis=0, tiled=True)
    living = parent >= 0
    source = jnp.maximum(parent, 0)
    kicked = (jnp.exp(field)[:, :, None] * column[source].astype(jnp.float32)).astype(jnp.bfloat16)
    new_walkers = jnp.where(living[:, None, None], kicked, jnp.zeros_like(kicked))
    theta = green_half(kicked)
    energy = jnp.zeros((slot_dev,), jnp.float32) + block_energy(
        theta, lax.all_gather(half_chol, "chol", axis=0, tiled=True)
    )
    energy = jnp.where(living, energy, 0.0)
    return (new_walkers, energy)


def solution(mesh):
    return jax.shard_map(
        body,
        mesh=mesh,
        in_specs=(
            P(("walk", "chol"), None, None),
            P("chol", None, None),
            P(("walk", "chol")),
            P(("walk", "chol"), None),
        ),
        out_specs=(P(("walk", "chol"), None, None), P(("walk", "chol"))),
        check_vma=False,
    )
```

profile of v0, /device:TPU:0, one launch (start us, length us, event | category | flops | bytes accessed | tf_op | source)
XLA Modules:
  0.0 217.5 jit_solution(15850261391445615935)
XLA Ops:
  7.2 0.0 all-gather.3.cloned.1.call-start
  7.2 0.7 all-gather.3.cloned.1.call-update
  7.9 0.0 all-gather.5.cloned.1.call-start
  7.9 0.7 all-gather.5.cloned.1.call-update
  8.6 0.9 exp.3
  9.5 0.7 broadcast_maximum_fusion
  10.2 0.6 iota_compare_fusion.1
  10.8 0.6 fusion.15
  11.4 0.7 fusion.16
  12.1 0.7 broadcast_compare_fusion
  12.7 45.9 %all-gather.3.cloned.1.call-done = bf16[12,2048,128]{2,1,0:T(8,128)(2,1)} async-done(((bf16[3,2048,128]{2,1,0:T(8,128)(2,1)}), bf16[12,2048,128]{2,1,0:T(8,128)(2,1)}) %all-gather.3.cloned.1.call-update) | async-done | bytes 6291472 | tf_op jit(solution)/shard_map/all_gather | solution.py:37
  58.7 5.5 %gather_fusion = bf16[6,2048,128]{2,1,0:T(8,128)(2,1)} fusion(bf16[12,2048,128]{2,1,0:T(8,128)(2,1)} %all-gather.3.cloned.1.call-done, s32[1024]{0:T(1024)S(1)} %pad_clamp_fusion), kind=kCustom, calls=%fused_computation | custom fusion | bytes 6291480 | tf_op jit(solution)/shard_map/gather | solution.py:40
  64.2 5.1 %broadcast_select_fusion = (bf16[6,2048,128]{2,1,0:T(8,128)(2,1)}, bf16[6,2048,128]{2,1,0:T(8,128)(2,1)S(1)}) fusion(pred[6]{0:T(512)(128)(4,1)S(1)} %broadcast_compare_fusion, bf16[6,2048,128]{2,1,0:T(8,128)(2,1)} %gather_fusion, f32[6,2048]{1,0:T(8,128)S(1)} %exp.3), kind=kLoop, calls=%fused_computation.11 | loop fusion | flops 6291456 | bytes 9486342 | tf_op jit(solution)/shard_map/jit(_where)/select_n | solution.py:41
  69.3 4.7 %copy.17 = f32[6,128,128]{0,2,1:T(8,128)} copy(f32[6,128,128]{2,1,0:T(8,128)S(1)} %slice_convert_fusion) | data formatting | bytes 786432 | tf_op jit(solution)/shard_map/slice | solution.py:12
  74.0 1.8 gather_fusion.1
  75.8 0.1 copy.18
  75.8 1.3 convolution_subtract_fusion.2
  77.1 1.4 fusion.5
  78.5 0.0 copy-done
  78.5 0.3 convolution_subtract_fusion.1
  78.9 0.5 fusion.17
  79.4 0.3 convolution_subtract_fusion
  79.7 0.5 fusion.18
  80.3 4.0 %convolution_convert_fusion = bf16[6,2048,128]{2,1,0:T(8,128)(2,1)} fusion(bf16[6,2048,128]{2,1,0:T(8,128)(2,1)S(1)} %get-tuple-element.7, f32[6,128,128]{2,1,0:T(8,128)S(1)} %fusion.18), kind=kOutput, calls=%fused_computation.9 | convolution fusion | flops 2417491968 | bytes 6684672 | tf_op jit(solution)/shard_map/wnk,wkj->wnj/dot_general | solution.py:24
  84.2 101.5 %all-gather.5.cloned.1.call-done = bf16[16,128,2048]{2,1,0:T(8,128)(2,1)} async-done(((bf16[2,128,2048]{2,1,0:T(8,128)(2,1)}), bf16[16,128,2048]{2,1,0:T(8,128)(2,1)}) %all-gather.5.cloned.1.call-update) | async-done | bytes 8388624 | tf_op jit(solution)/shard_map/all_gather | solution.py:44
  185.8 11.7 %fusion = f32[6,128,16,128]{3,1,2,0:T(8,128)} fusion(bf16[16,128,2048]{2,1,0:T(8,128)(2,1)} %all-gather.5.cloned.1.call-done, bf16[6,2048,128]{2,1,0:T(8,128)(2,1)} %convolution_convert_fusion), kind=kOutput, calls=%fused_computation.2 | convolution fusion | flops 6442450944 | bytes 17825792 | tf_op jit(solution)/shard_map/gin,wnj->wgij/dot_general | solution.py:29
  197.5 6.6 %copy.20 = f32[6,128,16,128]{1,3,2,0:T(8,128)} copy(f32[6,128,16,128]{3,1,2,0:T(8,128)} %fusion) | data formatting | bytes 12582912 | tf_op jit(solution)/shard_map/gin,wnj->wgij/dot_general | solution.py:29
  204.1 0.0 copy-done.1
  204.1 5.9 %fusion.3 = (f32[6,16]{1,0:T(8,128)S(1)}, f32[6,16]{1,0:T(8,128)S(1)}) fusion(f32[6,128,16,128]{1,3,2,0:T(8,128)} %copy.20, pred[128,128]{1,0:T(8,128)(4,1)S(1)} %copy-done.1, f32[6,128,16,128]{3,1,2,0:T(8,128)} %fusion), kind=kLoop, calls=%fused_computation.7 | loop fusion | flops 6291264 | bytes 12600064 | tf_op jit(solution)/shard_map/wgii->wg/reduce_sum | solution.py:30
  210.0 0.1 subtract_reduce_fusion
  210.1 0.0 copy-done.2
  210.1 0.5 multiply_select_fusion
  (6 shorter events, 0.0 us)
Async XLA Ops:
  7.2 51.5 %all-gather.3.cloned.1.call-start = ((), (), s32[]{:S(2)}) async-start(), calls=%async_computation | async-start | bytes 7864320 | tf_op jit(solution)/shard_map/all_gather | solution.py:37
  7.9 177.9 %all-gather.5.cloned.1.call-start = ((), (), s32[]{:S(2)}) async-start(), calls=%async_computation.1 | async-start | bytes 9437184 | tf_op jit(solution)/shard_map/all_gather | solution.py:44
  74.0 4.5 %copy-start = (f32[128,128]{1,0:T(8,128)S(1)}, f32[128,128]{1,0:T(8,128)}, u32[]{:S(2)}) copy-start(f32[128,128]{1,0:T(8,128)} %fusion.15) | copy-start | bytes 196612
  197.5 6.6 %copy-start.1 = (pred[128,128]{1,0:T(8,128)(4,1)S(1)}, pred[128,128]{1,0:T(8,128)(4,1)}, u32[]{:S(2)}) copy-start(pred[128,128]{1,0:T(8,128)(4,1)} %iota_compare_fusion.1) | copy-start | bytes 49156
  204.1 6.0 %copy-start.2 = (s32[6]{0:T(128)S(1)}, s32[6]{0:T(128)}, u32[]{:S(2)}) copy-start(s32[6]{0:T(128)} %param.6) | copy-start | bytes 76
Sparse Core Ops, SparseCore 0:
  9.6 49.0 all-gather.2
  60.8 124.9 all-gather.4
where the time goes:
time: 218 us; the launch traced here: 217 us
  waiting for transfers between devices  149 us (68%)
  matrix products  20.1 us (9%)
  local copies, waits for them, and re-layouts  19.5 us (9%)
  other arithmetic  14.8 us (7%)
  between operations  14.1 us (6%)
    all_gather x1, waiting for transfers between devices, body(): lax.all_gather(half_chol, 'chol', axis=0, tiled=True)  102 us
    all_gather x1, waiting for transfers between devices, body(): column = lax.all_gather(old_walkers, 'walk', axis=0, tiled=True)  45.9 us
    dot_general x1, matrix products, block_energy(): jnp.einsum('gin,wnj->wgij', vectors, theta, preferred_element_type=jnp.fl...  11.7 us
    dot_general x1, local copies, waits for them, and re-layouts, block_energy(): jnp.einsum('gin,wnj->wgij', vectors, theta, preferred_element_type=jnp.fl...  6.6 us
    reduce_sum x1, other arithmetic, block_energy(): traces = jnp.einsum('wgii->wg', blocks)  5.87 us
    gather x1, local copies, waits for them, and re-layouts, body(): column[source].astype(jnp.float32)  5.5 us
    select_n x1, other arithmetic, body(): jnp.where(living[:, None, None], kicked, jnp.zeros_like(kicked))  5.09 us
    slice x1, local copies, waits for them, and re-layouts, green_half(): intersection = widened[:, :electrons, :]  4.72 us
  transfers between devices with their start and end apart: 2, of which 2 were waited for; matrix products, arithmetic and copies ran while one was open for 14% of the time, Pallas kernels for 0%

commit v1 on v0

--- a/solution.py
+++ b/solution.py
@@ -4,6 +4,28 @@
 from jax.sharding import PartitionSpec as P
 
 ITERS = 3
+
+
+def joined_along(parts, dim):
+    dims = list(parts.shape[1:])
+    dims[dim] *= parts.shape[0]
+    return jnp.moveaxis(parts, 0, dim).reshape(dims)
+
+
+def doubled(x, axis):
+    length = lax.axis_size(axis)
+    parts = x[None]
+    for level in range(length.bit_length() - 1):
+        distance = 1 << level
+        other = lax.ppermute(parts, axis, [(i, i ^ distance) for i in range(length)])
+        both = jnp.stack([parts, other])
+        upper = lax.axis_index(axis) >> level & 1
+        parts = jnp.where(upper == 0, both, both[::-1]).reshape(-1, *x.shape)
+    return parts
+
+
+def gather_by_bits(x, axis, dim):
+    return joined_along(doubled(x, axis), dim)
 
 
 def green_half(walkers):
@@ -34,7 +56,7 @@
 
 def body(old_walkers, half_chol, parent, field):
     slot_dev = parent.shape[0]
-    column = lax.all_gather(old_walkers, "walk", axis=0, tiled=True)
+    column = gather_by_bits(old_walkers, "walk", 0)
     living = parent >= 0
     source = jnp.maximum(parent, 0)
     kicked = (jnp.exp(field)[:, :, None] * column[source].astype(jnp.float32)).astype(jnp.bfloat16)

time: 218 us -> 170 us (0.78)
  waiting for transfers between devices: 149 us -> 88.7 us
  other arithmetic: 14.8 us -> 24.4 us
  starting transfers between devices: 0.08 us -> 3.42 us
    all_gather x1, waiting for transfers between devices: 102 us -> 18.1 us  [body(): lax.all_gather(half_chol, 'chol', axis=0, tiled=True)]
    ppermute x0 -> x2, waiting for transfers between devices: none -> 70 us  [doubled(): lax.ppermute(parts, axis, [(i, i ^ distance) for i in range(length)])]
    all_gather x1 -> x0, waiting for transfers between devices: 45.9 us -> none  [body(): column = lax.all_gather(old_walkers, 'walk', axis=0, tiled=True)]
    another operation x0 -> x3, other arithmetic: none -> 6.91 us  [doubled(): both = jnp.stack([parts, other])]
    select_n x0 -> x1, other arithmetic: none -> 4.05 us  [doubled(): parts = jnp.where(upper == 0, both, both[::-1]).reshape(-1, *x.shape)]
    ppermute x0 -> x2, starting transfers between devices: none -> 3.38 us  [doubled(): lax.ppermute(parts, axis, [(i, i ^ distance) for i in range(length)])]
  transfers between devices with their start and end apart: 2 -> 3, of which waited for: 2 -> 3; matrix products, arithmetic and copies ran while one was open for 14% -> 23% of each run, Pallas kernels for 0% -> 0%
where the time goes in v1:
time: 170 us; the launch traced here: 169 us
  waiting for transfers between devices  88.7 us (52%)
  other arithmetic  24.4 us (14%)
  matrix products  20.1 us (12%)
  local copies, waits for them, and re-layouts  18.6 us (11%)
  between operations  14.2 us (8%)
  starting transfers between devices  3.42 us (2%)
    ppermute x2, waiting for transfers between devices, doubled(): lax.ppermute(parts, axis, [(i, i ^ distance) for i in range(length)])  70 us
    all_gather x1, waiting for transfers between devices, body(): lax.all_gather(half_chol, 'chol', axis=0, tiled=True)  18.1 us
    dot_general x1, matrix products, block_energy(): jnp.einsum('gin,wnj->wgij', vectors, theta, preferred_element_type=jnp.fl...  11.7 us
    another operation x3, other arithmetic, doubled(): both = jnp.stack([parts, other])  6.91 us
    dot_general x1, local copies, waits for them, and re-layouts, block_energy(): jnp.einsum('gin,wnj->wgij', vectors, theta, preferred_element_type=jnp.fl...  6.58 us
    reduce_sum x1, other arithmetic, block_energy(): traces = jnp.einsum('wgii->wg', blocks)  5.87 us
    gather x1, local copies, waits for them, and re-layouts, body(): column[source].astype(jnp.float32)  5.5 us
    select_n x1, other arithmetic, body(): jnp.where(living[:, None, None], kicked, jnp.zeros_like(kicked))  5.05 us
  transfers between devices with their start and end apart: 3, of which 3 were waited for; matrix products, arithmetic and copies ran while one was open for 23% of the time, Pallas kernels for 0%

profile of v1, /device:TPU:0, one launch (start us, length us, event | category | flops | bytes accessed | tf_op | source)
XLA Modules:
  0.0 169.5 jit_solution(14174605143107208521)
XLA Ops:
  7.2 0.0 all-gather.2.cloned.1.call-start
  7.2 0.7 all-gather.2.cloned.1.call-update
  7.9 0.5 collective-permute-start
  8.4 3.2 %collective-permute-done = bf16[1,3,2048,128]{3,2,1,0:T(8,128)(2,1)S(1)} collective-permute-done((bf16[1,3,2048,128]{3,2,1,0:T(8,128)(2,1)}, bf16[1,3,2048,128]{3,2,1,0:T(8,128)(2,1)S(1)}, u32[]{:S(2)}, u32[]{:S(2)}) %collective-permute-start) | collective-permute-done | bytes 1572896 | tf_op jit(solution)/shard_map/ppermute | solution.py:20
  11.7 1.7 %pad_maximum_fusion.1 = bf16[2,1,3,2048,128]{4,3,2,1,0:T(8,128)(2,1)S(1)} fusion(bf16[1,1,3,2048,128]{4,3,2,1,0:T(8,128)(2,1)S(1)} %bitcast.41, bf16[1,1,3,2048,128]{4,3,2,1,0:T(8,128)(2,1)} %bitcast.40), kind=kLoop, calls=%fused_computation.13 | loop fusion | flops 1572864 | bytes 6291456 | tf_op jit(solution)/shard_map/stack | solution.py:21
  13.4 0.0 copy-start.2
  13.4 2.7 %fusion.6 = (bf16[1,2,3,2048,128]{4,3,2,1,0:T(8,128)(2,1)S(1)}, bf16[2,3,2048,128]{3,2,1,0:T(8,128)(2,1)}) fusion(bf16[2,1,3,2048,128]{4,3,2,1,0:T(8,128)(2,1)S(1)} %pad_maximum_fusion.1, pred[]{:T(512)S(6)} %eq.26), kind=kLoop, calls=%fused_computation.17 | loop fusion | flops 1572864 | bytes 9437185 | tf_op jit(solution)/shard_map/stack;reshape | solution.py:21
  16.1 2.9 %collective-permute-start.1 = (bf16[2,3,2048,128]{3,2,1,0:T(8,128)(2,1)}, bf16[2,3,2048,128]{3,2,1,0:T(8,128)(2,1)}, u32[]{:S(2)}, u32[]{:S(2)}) collective-permute-start(bf16[2,3,2048,128]{3,2,1,0:T(8,128)(2,1)} %get-tuple-element.9), channel_id=1, source_target_pairs={{0,16},{8,24},{16,0},{24,8},{1,17},{9,25},{17,1},{25,9},{2,18},{10... | collective-permute-start | bytes 9437192 | tf_op jit(solution)/shard_map/ppermute | solution.py:20
  19.1 0.6 iota_compare_fusion.1
  19.7 0.6 fusion.17
  20.3 0.6 fusion.18
  21.0 66.8 %collective-permute-done.1 = bf16[2,3,2048,128]{3,2,1,0:T(8,128)(2,1)} collective-permute-done((bf16[2,3,2048,128]{3,2,1,0:T(8,128)(2,1)}, bf16[2,3,2048,128]{3,2,1,0:T(8,128)(2,1)}, u32[]{:S(2)}, u32[]{:S(2)}) %collective-permute-start.1) | collective-permute-done | bytes 3145760 | tf_op jit(solution)/shard_map/ppermute | solution.py:20
  87.7 2.5 %pad_maximum_fusion = bf16[2,2,3,2048,128]{4,3,2,1,0:T(8,128)(2,1)S(1)} fusion(bf16[1,2,3,2048,128]{4,3,2,1,0:T(8,128)(2,1)} %bitcast.5, bf16[1,2,3,2048,128]{4,3,2,1,0:T(8,128)(2,1)S(1)} %get-tuple-element.8), kind=kLoop, calls=%fused_computation.5 | loop fusion | flops 3145728 | bytes 12582912 | tf_op jit(solution)/shard_map/stack | solution.py:21
  90.2 4.0 %reverse_select_fusion = bf16[2,2,3,2048,128]{4,3,2,1,0:T(8,128)(2,1)} fusion(bf16[2,2,3,2048,128]{4,3,2,1,0:T(8,128)(2,1)S(1)} %pad_maximum_fusion, pred[]{:T(512)S(6)} %eq.25), kind=kLoop, calls=%fused_computation.2 | loop fusion | flops 3145728 | bytes 12582913 | tf_op jit(solution)/shard_map/jit(_where)/select_n | solution.py:23
  94.2 5.5 %gather_fusion = bf16[6,2048,128]{2,1,0:T(8,128)(2,1)} fusion(bf16[12,2048,128]{2,1,0:T(8,128)(2,1)} %bitcast.38, s32[1024]{0:T(1024)S(1)} %pad_clamp_fusion), kind=kCustom, calls=%fused_computation | custom fusion | bytes 6291480 | tf_op jit(solution)/shard_map/gather | solution.py:62
  99.7 5.1 %broadcast_select_fusion = (bf16[6,2048,128]{2,1,0:T(8,128)(2,1)}, bf16[6,2048,128]{2,1,0:T(8,128)(2,1)S(1)}) fusion(pred[6]{0:T(512)(128)(4,1)S(1)} %broadcast_compare_fusion, bf16[6,2048,128]{2,1,0:T(8,128)(2,1)} %gather_fusion, f32[6,2048]{1,0:T(8,128)S(1)} %exp.3), kind=kLoop, calls=%fused_computation.15 | loop fusion | flops 6291456 | bytes 9486342 | tf_op jit(solution)/shard_map/jit(_where)/select_n | solution.py:63
  104.8 4.7 %copy.17 = f32[6,128,128]{0,2,1:T(8,128)} copy(f32[6,128,128]{2,1,0:T(8,128)S(1)} %slice_convert_fusion) | data formatting | bytes 786432 | tf_op jit(solution)/shard_map/slice | solution.py:34
  109.5 1.8 %gather_fusion.1 = f32[128,6]{1,0:T(8,128)S(1)} fusion(f32[6,128,128]{0,2,1:T(8,128)} %copy.17, s32[128]{0:T(128)S(1)} %or_bitcast_fusion), kind=kCustom, calls=%fused_computation.1 | custom fusion | bytes 7168 | tf_op jit(solution)/shard_map/jit(diagonal)/gather | solution.py:36
  111.3 0.1 copy.18
  111.3 1.3 convolution_subtract_fusion.2
  112.6 1.4 fusion.7
  114.0 0.3 convolution_subtract_fusion.1
  114.4 0.5 fusion.19
  114.9 0.3 convolution_subtract_fusion
  115.2 0.5 fusion.20
  115.8 3.9 %convolution_convert_fusion = bf16[6,2048,128]{2,1,0:T(8,128)(2,1)} fusion(bf16[6,2048,128]{2,1,0:T(8,128)(2,1)S(1)} %get-tuple-element.7, f32[6,128,128]{2,1,0:T(8,128)S(1)} %fusion.20), kind=kOutput, calls=%fused_computation.12 | convolution fusion | flops 2417491968 | bytes 6684672 | tf_op jit(solution)/shard_map/wnk,wkj->wnj/dot_general | solution.py:46
  119.7 18.1 %all-gather.2.cloned.1.call-done = bf16[16,128,2048]{2,1,0:T(8,128)(2,1)} async-done(((bf16[2,128,2048]{2,1,0:T(8,128)(2,1)}), bf16[16,128,2048]{2,1,0:T(8,128)(2,1)}) %all-gather.2.cloned.1.call-update) | async-done | bytes 8388624 | tf_op jit(solution)/shard_map/all_gather | solution.py:66
  137.8 11.7 %fusion = f32[6,128,16,128]{3,1,2,0:T(8,128)} fusion(bf16[16,128,2048]{2,1,0:T(8,128)(2,1)} %all-gather.2.cloned.1.call-done, bf16[6,2048,128]{2,1,0:T(8,128)(2,1)} %convolution_convert_fusion), kind=kOutput, calls=%fused_computation.3 | convolution fusion | flops 6442450944 | bytes 17825792 | tf_op jit(solution)/shard_map/gin,wnj->wgij/dot_general | solution.py:51
  149.5 6.6 %copy.20 = f32[6,128,16,128]{1,3,2,0:T(8,128)} copy(f32[6,128,16,128]{3,1,2,0:T(8,128)} %fusion) | data formatting | bytes 12582912 | tf_op jit(solution)/shard_map/gin,wnj->wgij/dot_general | solution.py:51
  156.1 5.9 %fusion.3 = (f32[6,16]{1,0:T(8,128)S(1)}, f32[6,16]{1,0:T(8,128)S(1)}) fusion(f32[6,128,16,128]{1,3,2,0:T(8,128)} %copy.20, pred[128,128]{1,0:T(8,128)(4,1)S(1)} %copy-done.1, f32[6,128,16,128]{3,1,2,0:T(8,128)} %fusion), kind=kLoop, calls=%fused_computation.9 | loop fusion | flops 6291264 | bytes 12600064 | tf_op jit(solution)/shard_map/wgii->wg/reduce_sum | solution.py:52
  162.0 0.1 subtract_reduce_fusion
  162.1 0.5 multiply_select_fusion
  (13 shorter events, 0.1 us)
Async XLA Ops:
  7.2 130.6 %all-gather.2.cloned.1.call-start = ((), (), s32[]{:S(2)}) async-start(), calls=%async_computation | async-start | bytes 9437184 | tf_op jit(solution)/shard_map/all_gather | solution.py:66
  7.9 3.8 %collective-permute-start = (bf16[1,3,2048,128]{3,2,1,0:T(8,128)(2,1)}, bf16[1,3,2048,128]{3,2,1,0:T(8,128)(2,1)S(1)}, u32[]{:S(2)}, u32[]{:S(2)}) collective-permute-start(bf16[1,3,2048,128]{3,2,1,0:T(8,128)(2,1)} %bitcast.39), channel_id=1, source_target_pairs={{0,8},{8,0},{16,24},{24,16},{1,9},{9,1},{17,25},{25,17},{2,10},{10... | collective-permute-start | bytes 4718600 | tf_op jit(solution)/shard_map/ppermute | solution.py:20
  13.4 5.6 %copy-start.2 = (f32[6,2048]{1,0:T(8,128)S(1)}, f32[6,2048]{1,0:T(8,128)}, u32[]{:S(2)}) copy-start(f32[6,2048]{1,0:T(8,128)} %param.7) | copy-start | bytes 147460
  13.4 5.7 %copy-start.3 = (s32[6]{0:T(128)S(1)}, s32[6]{0:T(128)}, u32[]{:S(2)}) copy-start(s32[6]{0:T(128)} %param.6) | copy-start | bytes 76
  16.1 71.6 %collective-permute-start.1 = (bf16[2,3,2048,128]{3,2,1,0:T(8,128)(2,1)}, bf16[2,3,2048,128]{3,2,1,0:T(8,128)(2,1)}, u32[]{:S(2)}, u32[]{:S(2)}) collective-permute-start(bf16[2,3,2048,128]{3,2,1,0:T(8,128)(2,1)} %get-tuple-element.9), channel_id=1, source_target_pairs={{0,16},{8,24},{16,0},{24,8},{1,17},{9,25},{17,1},{25,9},{2,18},{10... | collective-permute-start | bytes 9437192 | tf_op jit(solution)/shard_map/ppermute | solution.py:20
  109.5 4.5 %copy-start = (f32[128,128]{1,0:T(8,128)S(1)}, f32[128,128]{1,0:T(8,128)}, u32[]{:S(2)}) copy-start(f32[128,128]{1,0:T(8,128)} %fusion.17) | copy-start | bytes 196612
  149.5 6.6 %copy-start.1 = (pred[128,128]{1,0:T(8,128)(4,1)S(1)}, pred[128,128]{1,0:T(8,128)(4,1)}, u32[]{:S(2)}) copy-start(pred[128,128]{1,0:T(8,128)(4,1)} %iota_compare_fusion.1) | copy-start | bytes 49156
Sparse Core Ops, SparseCore 0:
  10.1 127.6 all-gather.1
